TPU v7x, 32 devices: a whole 2x2x4 slice. The times are simulated.
32 devices in a mesh: seq: 8 (over y, x, core), head: 4 (over z).
Axes of the slice: x: 2, y: 2, z: 4, core: 2. Of those that a mesh axis runs over, the one named last changes fastest.
Arguments:
- queries: bfloat16 [4096, 64, 128], P(('seq', 'head')), may hold values from -36 to 36
- keys: bfloat16 [4096, 8, 128], P(('seq', 'head')), may hold values from -6 to 6
- values: bfloat16 [4096, 8, 128], P(('seq', 'head')), may hold values from -6 to 6
- output_gradient: bfloat16 [4096, 64, 128], P(('seq', 'head')), may hold values from -6 to 6
- global_blocks: int32 [2], replicated, may hold values from 0 to 31, as said below
- random_blocks: int32 [32, 3], replicated, may hold values from 0 to 31, as said below
Outputs:
- out: bfloat16 [4096, 64, 128], P(('seq', 'head'))
- grad_queries: bfloat16 [4096, 64, 128], P(('seq', 'head'))
- grad_keys: bfloat16 [4096, 8, 128], P(('seq', 'head'))
- grad_values: bfloat16 [4096, 8, 128], P(('seq', 'head'))
Inputs may be any that keep to these rules, and one draw needn't show every extreme that they name: `global_blocks`: the two blocks differ; one of them is the last block, 31. `random_blocks`: call 4 consecutive blocks starting at a multiple of 4 a group. The entries listed by a group's query blocks never lie in that group's own blocks, and at most 2 of them lie in any one other group; in every group some other group is hit exactly 2 times.
All inputs are finite; a program needn't handle non-finite values.
Results may differ from a plain program's by a relative error of at most 0.035.
Values may be sent and summed in bfloat16 or wider, within the bound.
No kernel may reach another device: no remote copies, remote signals or barrier semaphores. Data moves between devices by JAX's collectives and lax.ppermute only.
A program may use at most 128 MiB of HBM per device.

v0:
```python
import math
import jax
import jax.numpy as jnp
from jax import lax
from jax.sharding import PartitionSpec as P

BLOCK_TOKENS = 128


def padded(shard, sides, width):
    for axis, dim in sides:
        count, length = (lax.axis_size(axis), shard.shape[dim])
        up = [(i, (i + 1) % count) for i in range(count - 1)]
        down = [(j, i) for i, j in up]
        last = lax.slice_in_dim(shard, length - width, length, axis=dim)
        leading = lax.slice_in_dim(shard, 0, width, axis=dim)
        before = lax.ppermute(last, axis, up)
        after = lax.ppermute(leading, axis, down)
        shard = jnp.concatenate([before, shard, after], axis=dim)
    return shard


def from_root(block, axis, owner):
    block = jnp.where(lax.axis_index(axis) == owner, block, jnp.zeros_like(block))
    return lax.psum(block, axis)


def per_device(queries, keys, values, output_gradient, global_blocks, random_blocks):
    query_loc, key_loc, value_loc, grad_loc = (
        lax.all_to_all(queries, "head", split_axis=1, concat_axis=0, tiled=True),
        lax.all_to_all(keys, "head", split_axis=1, concat_axis=0, tiled=True),
        lax.all_to_all(values, "head", split_axis=1, concat_axis=0, tiled=True),
        lax.all_to_all(output_gradient, "head", split_axis=1, concat_axis=0, tiled=True),
    )
    shard_len, heads_q, head_width = query_loc.shape
    heads_kv = key_loc.shape[1]
    heads_per_group = heads_q // heads_kv
    kv_width = heads_kv * head_width
    blocks = shard_len // BLOCK_TOKENS
    seq_count = lax.axis_size("seq")
    own_index = lax.axis_index("seq")
    block_total_count = seq_count * blocks
    capacity = (3 * blocks + seq_count - 2) // (seq_count - 1)
    entry_count = 3 * blocks
    score_scale = 1.0 / math.sqrt(head_width)
    kv_pair = jnp.stack(
        [key_loc.reshape(shard_len, kv_width), value_loc.reshape(shard_len, kv_width)]
    )
    extended = padded(kv_pair, (("seq", 1),), BLOCK_TOKENS)
    kv_tiles = kv_pair.reshape(2, blocks, BLOCK_TOKENS, kv_width).transpose(1, 0, 2, 3)
    global_owner = global_blocks // blocks
    global_offset = global_blocks % blocks
    own_global = (jnp.arange(blocks)[None, :] == global_offset[:, None]) & (
        global_owner == own_index
    )[:, None]
    received_rows = []
    for global_slot in range(2):
        candidate = lax.dynamic_index_in_dim(
            kv_tiles, global_offset[global_slot], 0, keepdims=False
        )
        received_rows.append(from_root(candidate, "seq", global_owner[global_slot]))
    global_tiles = jnp.stack(received_rows)
    all_entries = (
        random_blocks.reshape(seq_count, blocks, 3)
        .transpose(0, 2, 1)
        .reshape(seq_count, entry_count)
    )
    all_owner = all_entries // blocks
    entry_ids = jnp.arange(entry_count)
    entry_earlier = entry_ids[None, :] < entry_ids[:, None]
    all_rank = jnp.sum(
        (all_owner[:, :, None] == all_owner[:, None, :]) & entry_earlier[None], axis=2
    )
    my_entries = lax.dynamic_index_in_dim(all_entries, own_index, 0, keepdims=False)
    my_owner = lax.dynamic_index_in_dim(all_owner, own_index, 0, keepdims=False)
    my_rank = lax.dynamic_index_in_dim(all_rank, own_index, 0, keepdims=False)
    my_slot = my_owner * capacity + my_rank
    owned_here = (all_owner == own_index)[:, :, None] & (
        all_rank[:, :, None] == jnp.arange(capacity)[None, None, :]
    )
    offset_match = (all_entries % blocks)[:, :, None] == jnp.arange(blocks)[None, None, :]
    selector = jnp.einsum(
        "tec,teo->tco",
        owned_here.astype(jnp.bfloat16),
        offset_match.astype(jnp.bfloat16),
        preferred_element_type=jnp.float32,
    ).astype(jnp.bfloat16)
    everything = lax.all_gather(kv_pair, "seq", axis=1, tiled=True)
    tiled_all = everything.reshape(2, block_total_count, BLOCK_TOKENS, kv_width)
    random_tiles = jnp.take(tiled_all, my_entries, axis=1).transpose(1, 0, 2, 3)
    random_by_block = random_tiles.reshape(3, blocks, 2, BLOCK_TOKENS, kv_width).transpose(
        1, 0, 2, 3, 4
    )
    block_ids = own_index * blocks + jnp.arange(blocks)
    listed = jnp.concatenate(
        [
            jnp.stack([block_ids - 1, block_ids, block_ids + 1], axis=1),
            jnp.broadcast_to(global_blocks[None, :], (blocks, 2)),
            my_entries.reshape(3, blocks).T,
        ],
        axis=1,
    )
    inside = (listed >= 0) & (listed < block_total_count)
    tile_ids = jnp.arange(8)
    tile_earlier = tile_ids[None, :] < tile_ids[:, None]
    repeat = jnp.any((listed[:, :, None] == listed[:, None, :]) & tile_earlier[None], axis=2)
    live = inside & jnp.logical_not(repeat)

    def attend(unused_state, inputs):
        query_blk, grad_blk, random_blk, live_row, position = inputs
        near_tiles = lax.dynamic_slice_in_dim(
            extended, position * BLOCK_TOKENS, 3 * BLOCK_TOKENS, 1
        )
        near_tiles = near_tiles.reshape(2, 3, BLOCK_TOKENS, kv_width).transpose(1, 0, 2, 3)
        all_tiles = jnp.concatenate([near_tiles, global_tiles, random_blk], axis=0)
        key_t = all_tiles[:, 0].reshape(8, BLOCK_TOKENS, heads_kv, head_width)
        value_t = all_tiles[:, 1].reshape(8, BLOCK_TOKENS, heads_kv, head_width)
        query_grid = query_blk.reshape(BLOCK_TOKENS, heads_kv, heads_per_group, head_width)
        grad_grid = grad_blk.reshape(BLOCK_TOKENS, heads_kv, heads_per_group, head_width)
        scores = (
            jnp.einsum("qkgd,tbkd->kgqtb", query_grid, key_t, preferred_element_type=jnp.float32)
            * score_scale
        )
        scores = jnp.where(live_row[None, None, None, :, None], scores, -jnp.inf)
        row_max = jnp.max(scores, axis=(3, 4), keepdims=True)
        expo = jnp.exp(scores - row_max)
        attn_prob = expo / jnp.sum(expo, axis=(3, 4), keepdims=True)
        prob_low = attn_prob.astype(jnp.bfloat16)
        attended = jnp.einsum(
            "kgqtb,tbkd->qkgd", prob_low, value_t, preferred_element_type=jnp.float32
        )
        out_low = attended.astype(jnp.bfloat16)
        row_delta = jnp.sum(grad_grid.astype(jnp.float32) * out_low.astype(jnp.float32), axis=-1)
        grad_prob = jnp.einsum(
            "qkgd,tbkd->kgqtb", grad_grid, value_t, preferred_element_type=jnp.float32
        )
        grad_score = attn_prob * (
            grad_prob - jnp.transpose(row_delta, (1, 2, 0))[:, :, :, None, None]
        )
        score_low = grad_score.astype(jnp.bfloat16)
        query_grad = (
            jnp.einsum("kgqtb,tbkd->qkgd", score_low, key_t, preferred_element_type=jnp.float32)
            * score_scale
        )
        key_grad = (
            jnp.einsum(
                "kgqtb,qkgd->tbkd", score_low, query_grid, preferred_element_type=jnp.float32
            )
            * score_scale
        )
        value_grad = jnp.einsum(
            "kgqtb,qkgd->tbkd", prob_low, grad_grid, preferred_element_type=jnp.float32
        )
        tile_terms = jnp.stack(
            [
                key_grad.reshape(8, BLOCK_TOKENS, kv_width),
                value_grad.reshape(8, BLOCK_TOKENS, kv_width),
            ],
            axis=1,
        )
        return (
            unused_state,
            (
                out_low.reshape(BLOCK_TOKENS, heads_q, head_width),
                query_grad.astype(jnp.bfloat16).reshape(BLOCK_TOKENS, heads_q, head_width),
                tile_terms,
            ),
        )

    unused_final, (output_block_rows, query_gradient_rows, tile_grads) = lax.scan(
        attend,
        0,
        (
            query_loc.reshape(blocks, BLOCK_TOKENS, heads_q, head_width),
            grad_loc.reshape(blocks, BLOCK_TOKENS, heads_q, head_width),
            random_by_block,
            live,
            jnp.arange(blocks),
        ),
    )
    pad_spec_low = ((0, 2), (0, 0), (0, 0), (0, 0))
    pad_spec_mid = ((1, 1), (0, 0), (0, 0), (0, 0))
    pad_spec_high = ((2, 0), (0, 0), (0, 0), (0, 0))
    window_sum = (
        jnp.pad(tile_grads[:, 0], pad_spec_low)
        + jnp.pad(tile_grads[:, 1], pad_spec_mid)
        + jnp.pad(tile_grads[:, 2], pad_spec_high)
    )
    rims = jnp.concatenate([window_sum[0], window_sum[blocks + 1]], axis=1)
    returned_rims = padded(rims.astype(jnp.bfloat16), (("seq", 1),), BLOCK_TOKENS).astype(
        rims.dtype
    )
    interior = window_sum[1 : blocks + 1]
    interior = (
        interior.at[0]
        .add(returned_rims[:, :BLOCK_TOKENS])
        .at[blocks - 1]
        .add(returned_rims[:, 3 * BLOCK_TOKENS :])
    )
    global_terms = jnp.sum(tile_grads[:, 3:5], axis=0)
    global_total = lax.psum(global_terms.astype(jnp.bfloat16), "seq").astype(jnp.float32)
    own_weight = own_global.astype(jnp.float32)[:, :, None, None, None]
    interior = interior + jnp.sum(own_weight * global_total[:, None], axis=0)
    random_terms = (
        tile_grads[:, 5:8]
        .transpose(1, 0, 2, 3, 4)
        .reshape(entry_count, 2, BLOCK_TOKENS, kv_width)
        .astype(jnp.bfloat16)
    )
    slot_onehot = (my_slot[:, None] == jnp.arange(seq_count * capacity)[None, :]).astype(
        jnp.bfloat16
    )
    back_buffer = jnp.einsum(
        "es,exbw->sxbw", slot_onehot, random_terms, preferred_element_type=jnp.float32
    ).astype(jnp.bfloat16)
    returned_terms = lax.all_to_all(back_buffer, "seq", split_axis=0, concat_axis=0, tiled=True)
    interior = interior + jnp.einsum(
        "tco,tcxbw->oxbw",
        selector,
        returned_terms.reshape(seq_count, capacity, 2, BLOCK_TOKENS, kv_width),
        preferred_element_type=jnp.float32,
    )
    kv_grad = interior.transpose(1, 0, 2, 3).reshape(2, shard_len, kv_width).astype(jnp.bfloat16)
    out_all = output_block_rows.reshape(shard_len, heads_q, head_width)
    query_grad_all = query_gradient_rows.reshape(shard_len, heads_q, head_width)
    key_grad_all = kv_grad[0].reshape(shard_len, heads_kv, head_width)
    value_grad_all = kv_grad[1].reshape(shard_len, heads_kv, head_width)
    return (
        lax.all_to_all(out_all, "head", split_axis=0, concat_axis=1, tiled=True),
        lax.all_to_all(query_grad_all, "head", split_axis=0, concat_axis=1, tiled=True),
        lax.all_to_all(key_grad_all, "head", split_axis=0, concat_axis=1, tiled=True),
        lax.all_to_all(value_grad_all, "head", split_axis=0, concat_axis=1, tiled=True),
    )


def solution(mesh):
    placed = (
        P(("seq", "head"), None, None),
        P(("seq", "head"), None, None),
        P(("seq", "head"), None, None),
        P(("seq", "head"), None, None),
        P(),
        P(),
    )
    return jax.shard_map(
        per_device,
        mesh=mesh,
        in_specs=placed,
        out_specs=(
            P(("seq", "head"), None, None),
            P(("seq", "head"), None, None),
            P(("seq", "head"), None, None),
            P(("seq", "head"), None, None),
        ),
        check_vma=False,
    )
```

profile of v0, /device:TPU:0, one launch (start us, length us, event | category | flops | bytes accessed | tf_op | source)
XLA Modules:
  0.0 494.7 jit_solution(17608688807124787782)
XLA Ops:
  8.9 6.3 %all-to-all-start = ((bf16[128,8,128]{2,0,1:T(8,128)(2,1)}), bf16[128,8,128]{2,0,1:T(8,128)(2,1)S(1)}, u32[]{:S(2)}, u32[]{:S(2)}) async-start(bf16[128,8,128]{2,0,1:T(8,128)(2,1)} %copy.314), calls=%async_computation | async-start | bytes 524288 | tf_op jit(solution)/shard_map/all_to_all | solution.py:31
  16.9 7.2 %all-to-all-done = bf16[128,8,128]{2,0,1:T(8,128)(2,1)S(1)} async-done(((bf16[128,8,128]{2,0,1:T(8,128)(2,1)}), bf16[128,8,128]{2,0,1:T(8,128)(2,1)S(1)}, u32[]{:S(2)}, u32[]{:S(2)}) %all-to-all-start) | async-done | bytes 262176 | tf_op jit(solution)/shard_map/all_to_all | solution.py:31
  24.1 3.4 all-to-all-start.1
  28.1 6.5 %all-to-all-done.1 = bf16[128,8,128]{2,0,1:T(8,128)(2,1)S(1)} async-done(((bf16[128,8,128]{2,0,1:T(8,128)(2,1)}), bf16[128,8,128]{2,0,1:T(8,128)(2,1)S(1)}, u32[]{:S(2)}, u32[]{:S(2)}) %all-to-all-start.1) | async-done | bytes 262176 | tf_op jit(solution)/shard_map/all_to_all | solution.py:32
  38.5 3.7 all-to-all-start.3
  45.5 4.3 copy.322
  50.4 37.3 %all-to-all-done.3 = bf16[128,64,128]{2,0,1:T(8,128)(2,1)S(1)} async-done(((bf16[128,64,128]{2,0,1:T(8,128)(2,1)}), bf16[128,64,128]{2,0,1:T(8,128)(2,1)S(1)}, u32[]{:S(2)}, u32[]{:S(2)}) %all-to-all-start.3) | async-done | bytes 2097184 | tf_op jit(solution)/shard_map/all_to_all | solution.py:33
  87.7 4.5 all-to-all-start.2
  113.7 47.8 %all-reduce.9.cloned.1.call-done = (bf16[1,2,128,256]{3,2,1,0:T(8,128)(2,1)}, bf16[1,2,128,256]{3,2,0,1:T(8,128)(2,1)}) async-done(((bf16[1,2,128,256]{3,2,1,0:T(8,128)(2,1)}, bf16[1,2,128,256]{3,2,0,1:T(8,128)(2,1)}), (bf16[1,2,128,256]{3,2,1,0:T(8,128)(2,1)}, bf16[1,2,128,256]{3,2,0,1:T(8,128)(2,1)})) %all-reduce.9.cloned.1.call-update) | async-done | bytes 262160 | tf_op jit(solution)/shard_map/psum | solution.py:25
  161.4 105.5 %while.16 = (s32[]{:T(128)}, bf16[4,128,16,128]{3,2,1,0:T(8,128)(2,1)}, bf16[4,128,16,128]{3,2,1,0:T(8,128)(2,1)}, f32[4,8,2,128,256]{3,4,1,2,0:T(8,128)}, s32[4...) while((s32[]{:T(128)}, ...), condition=%wide.region_7.8_spmd, body=%wide.region_3.7_spmd.sunk | while | flops 3265259520 | bytes 89202968 | solution.py:170
  177.6 3.2 fusion.115
  204.0 3.2 fusion.115
  230.3 3.2 fusion.115
  256.7 3.2 fusion.115
  266.9 9.1 %copy.331 = f32[4,8,2,128,256]{4,3,2,0,1:T(8,128)} copy(f32[4,8,2,128,256]{3,4,1,2,0:T(8,128)} %get-tuple-element.94) | data formatting | bytes 16777216 | tf_op jit(solution)/shard_map/while | solution.py:170
  281.3 3.6 all-to-all-start.6
  298.7 3.8 scatter-add.9
  302.5 50.8 %all-reduce.7.cloned.1.call-done = bf16[2,2,128,256]{2,3,0,1:T(8,128)(2,1)} async-done(((bf16[2,2,128,256]{2,3,0,1:T(8,128)(2,1)}), bf16[2,2,128,256]{2,3,0,1:T(8,128)(2,1)}) %all-reduce.7.cloned.1.call-update) | async-done | bytes 262160 | tf_op jit(solution)/shard_map/psum | solution.py:201
  361.7 4.6 all-to-all-start.8
  366.4 8.1 %all-to-all-done.8 = bf16[512,2,128]{2,1,0:T(2,128)(2,1)S(1)} async-done(((bf16[512,2,128]{2,1,0:T(2,128)(2,1)}), bf16[512,2,128]{2,1,0:T(2,128)(2,1)S(1)}, u32[]{:S(2)}, u32[]{:S(2)}) %all-to-all-start.8) | async-done | bytes 262176 | tf_op jit(solution)/shard_map/all_to_all | solution.py:232
  374.5 10.4 %all_to_all.137 = bf16[512,2,128]{2,1,0:T(2,128)(2,1)S(1)} all-to-all(bf16[512,2,128]{2,1,0:T(2,128)(2,1)S(1)} %reshape_squeeze.6), channel_id=1, replica_groups=mesh['seq'=8,'head'=4] {'head'}, dimensions={0} | all-to-all | bytes 524288 | tf_op jit(solution)/shard_map/all_to_all | solution.py:231
  384.9 50.3 %all_to_all.138 = bf16[512,16,128]{2,1,0:T(8,128)(2,1)} all-to-all(bf16[512,16,128]{2,1,0:T(8,128)(2,1)S(1)} %bitcast.276), channel_id=1, replica_groups=mesh['seq'=8,'head'=4] {'head'}, dimensions={0} | all-to-all | bytes 4194304 | tf_op jit(solution)/shard_map/all_to_all | solution.py:230
  435.3 3.6 all-to-all-start.4
  442.8 43.4 %all-to-all-done.4 = bf16[512,16,128]{2,1,0:T(8,128)(2,1)S(1)} async-done(((bf16[512,16,128]{2,1,0:T(8,128)(2,1)}), bf16[512,16,128]{2,1,0:T(8,128)(2,1)S(1)}, u32[]{:S(2)}, u32[]{:S(2)}) %all-to-all-start.4) | async-done | bytes 2097184 | tf_op jit(solution)/shard_map/all_to_all | solution.py:229
  (225 shorter events, 150.4 us)
Async XLA Ops:
  8.9 15.3 %all-to-all-start = ((bf16[128,8,128]{2,0,1:T(8,128)(2,1)}), bf16[128,8,128]{2,0,1:T(8,128)(2,1)S(1)}, u32[]{:S(2)}, u32[]{:S(2)}) async-start(bf16[128,8,128]{2,0,1:T(8,128)(2,1)} %copy.314), calls=%async_computation | async-start | bytes 524288 | tf_op jit(solution)/shard_map/all_to_all | solution.py:31
  16.9 18.9 %copy-start.3 = (bf16[128,64,128]{2,1,0:T(8,128)(2,1)S(1)}, bf16[128,64,128]{2,1,0:T(8,128)(2,1)}, u32[]{:S(2)}) copy-start(bf16[128,64,128]{2,1,0:T(8,128)(2,1)} %param.15) | copy-start | bytes 6291460
  24.1 10.4 %all-to-all-start.1 = ((bf16[128,8,128]{2,0,1:T(8,128)(2,1)}), bf16[128,8,128]{2,0,1:T(8,128)(2,1)S(1)}, u32[]{:S(2)}, u32[]{:S(2)}) async-start(bf16[128,8,128]{2,0,1:T(8,128)(2,1)} %copy.316), calls=%async_computation.1 | async-start | bytes 524288 | tf_op jit(solution)/shard_map/all_to_all | solution.py:32
  27.5 81.9 %all-gather.2.cloned.1.call-start = ((), (), s32[]{:S(2)}) async-start(), calls=%async_computation.9 | async-start | bytes 4718592 | tf_op jit(solution)/shard_map/all_gather | solution.py:88
  38.5 3.8 copy-start.14
  38.5 49.2 %all-to-all-start.3 = ((bf16[128,64,128]{2,0,1:T(8,128)(2,1)}), bf16[128,64,128]{2,0,1:T(8,128)(2,1)S(1)}, u32[]{:S(2)}, u32[]{:S(2)}) async-start(bf16[128,64,128]{2,0,1:T(8,128)(2,1)} %copy.323), calls=%async_computation.3 | async-start | bytes 4194304 | tf_op jit(solution)/shard_map/all_to_all | solution.py:33
  42.3 7.5 %copy-start.9 = (s32[2]{0:T(128)}, s32[2]{0:T(128)S(1)}, u32[]{:S(2)}) copy-start(s32[2]{0:T(128)S(1)} %and_select_fusion) | copy-start | bytes 28
  50.4 43.6 %copy-start.13 = (s32[32,3]{0,1:T(4,128)S(1)}, s32[32,3]{0,1:T(4,128)}, u32[]{:S(2)}) copy-start(s32[32,3]{0,1:T(4,128)} %param.17) | copy-start | bytes 1156
  50.4 48.5 %copy-start.2 = (bf16[2,512,256]{2,1,0:T(8,128)(2,1)S(1)}, bf16[2,512,256]{2,1,0:T(8,128)(2,1)}, u32[]{:S(2)}) copy-start(bf16[2,512,256]{2,1,0:T(8,128)(2,1)} %copy-done.1) | copy-start | bytes 1572868
  87.7 73.8 %all-to-all-start.2 = ((bf16[128,64,128]{2,0,1:T(8,128)(2,1)}), bf16[128,64,128]{2,0,1:T(8,128)(2,1)}, u32[]{:S(2)}, u32[]{:S(2)}) async-start(bf16[128,64,128]{2,0,1:T(8,128)(2,1)} %copy.322), calls=%async_computation.2 | async-start | bytes 4194304 | tf_op jit(solution)/shard_map/all_to_all | solution.py:30
  92.2 69.3 %all-reduce.9.cloned.1.call-start = ((), (), s32[]{:S(2)}) async-start(), calls=%async_computation.11 | async-start | bytes 524288 | tf_op jit(solution)/shard_map/psum | solution.py:25
  99.6 3.4 collective-permute-start
  100.8 5.0 %collective-permute-start.1 = (bf16[2,128,256]{2,1,0:T(8,128)(2,1)S(1)}, bf16[2,128,256]{2,1,0:T(8,128)(2,1)S(1)}, u32[]{:S(2)}, u32[]{:S(2)}) collective-permute-start(bf16[2,128,256]{2,1,0:T(8,128)(2,1)S(1)} %get-tuple-element.249), channel_id=1, source_target_pairs={{4,0},{8,4},{12,8},{16,12},{20,16},{24,20},{28,24},{5,1},{9,5},{13... | collective-permute-start | bytes 393224 | tf_op jit(solution)/shard_map/ppermute | solution.py:18
  281.3 3.7 copy-start.15
  281.3 3.8 copy-start.8
  281.3 3.8 copy-start.11
  281.3 3.8 copy-start.16
  281.3 76.3 %all-to-all-start.6 = ((bf16[16,2,128,256]{3,2,1,0:T(8,128)(2,1)}), bf16[16,2,128,256]{3,2,1,0:T(8,128)(2,1)S(1)}, u32[]{:S(2)}, u32[]{:S(2)}) async-start(bf16[16,2,128,256]{3,2,1,0:T(8,128)(2,1)} %copy.347), calls=%async_computation.6 | async-start | bytes 4194304 | tf_op jit(solution)/shard_map/all_to_all | solution.py:216
  284.9 68.4 %all-reduce.7.cloned.1.call-start = ((), (), s32[]{:S(2)}) async-start(), calls=%async_computation.10 | async-start | bytes 524288 | tf_op jit(solution)/shard_map/psum | solution.py:201
  288.9 7.4 %collective-permute-start.2 = (bf16[2,128,256]{2,1,0:T(8,128)(2,1)S(1)}, bf16[2,128,256]{2,1,0:T(8,128)(2,1)S(1)}, u32[]{:S(2)}, u32[]{:S(2)}) collective-permute-start(bf16[2,128,256]{2,1,0:T(8,128)(2,1)S(1)} %get-tuple-element.242), channel_id=1, source_target_pairs={{0,4},{4,8},{8,12},{12,16},{16,20},{20,24},{24,28},{1,5},{5,9},{9,... | collective-permute-start | bytes 393224 | tf_op jit(solution)/shard_map/ppermute | solution.py:17
  291.2 5.2 %collective-permute-start.3 = (bf16[2,128,256]{2,1,0:T(8,128)(2,1)S(1)}, bf16[2,128,256]{2,1,0:T(8,128)(2,1)S(1)}, u32[]{:S(2)}, u32[]{:S(2)}) collective-permute-start(bf16[2,128,256]{2,1,0:T(8,128)(2,1)S(1)} %get-tuple-element.243), channel_id=1, source_target_pairs={{4,0},{8,4},{12,8},{16,12},{20,16},{24,20},{28,24},{5,1},{9,5},{13... | collective-permute-start | bytes 393224 | tf_op jit(solution)/shard_map/ppermute | solution.py:18
  360.7 24.2 %copy-start.4 = (bf16[4,128,16,128]{3,2,1,0:T(8,128)(2,1)S(1)}, bf16[4,128,16,128]{3,2,1,0:T(8,128)(2,1)}, u32[]{:S(2)}) copy-start(bf16[4,128,16,128]{3,2,1,0:T(8,128)(2,1)} %get-tuple-element.93) | copy-start | bytes 6291460
  361.7 12.8 %all-to-all-start.8 = ((bf16[512,2,128]{2,1,0:T(2,128)(2,1)}), bf16[512,2,128]{2,1,0:T(2,128)(2,1)S(1)}, u32[]{:S(2)}, u32[]{:S(2)}) async-start(bf16[512,2,128]{2,1,0:T(2,128)(2,1)} %reshape_squeeze.7), calls=%async_computation.8 | async-start | bytes 524288 | tf_op jit(solution)/shard_map/all_to_all | solution.py:232
  435.3 50.9 %all-to-all-start.4 = ((bf16[512,16,128]{2,1,0:T(8,128)(2,1)}), bf16[512,16,128]{2,1,0:T(8,128)(2,1)S(1)}, u32[]{:S(2)}, u32[]{:S(2)}) async-start(bf16[512,16,128]{2,1,0:T(8,128)(2,1)} %bitcast.277), calls=%async_computation.4 | async-start | bytes 4194304 | tf_op jit(solution)/shard_map/all_to_all | solution.py:229
  (7 other events, 12.7 us)
Sparse Core Ops, SparseCore 0:
  35.9 36.1 all-gather.1
  103.1 58.3 all-reduce.8
  295.1 58.1 all-reduce.6
where the time goes:
time: 497 us; the launch traced here: 495 us
  waiting for transfers between devices  204 us (41%)
  local copies, waits for them, and re-layouts  85.5 us (17%)
  blocking collectives  60.8 us (12%)
  matrix products  46.3 us (9%)
  other arithmetic  39.6 us (8%)
  starting transfers between devices  36.1 us (7%)
  between operations  19.4 us (4%)
    psum x1, waiting for transfers between devices, per_device(): lax.psum(global_terms.astype(jnp.bfloat16), 'seq').astype(jnp.float32)  50.8 us
    all_to_all x1, blocking collectives, per_device(): lax.all_to_all(query_grad_all, 'head', split_axis=0, concat_axis=1, tiled...  50.3 us
    psum x1, waiting for transfers between devices, from_root(): return lax.psum(block, axis)  47.8 us
    all_to_all x1, waiting for transfers between devices, per_device(): lax.all_to_all(out_all, 'head', split_axis=0, concat_axis=1, tiled=True)  43.4 us
    all_to_all x1, waiting for transfers between devices, per_device(): lax.all_to_all(output_gradient, 'head', split_axis=1, concat_axis=0, tile...  37.3 us
    unnamed x42, local copies, waits for them, and re-layouts  13.2 us
    dot_general x4, matrix products, attend(): jnp.einsum('qkgd,tbkd->kgqtb', grad_grid, value_t, preferred_element_type...  13 us
    dynamic_update_slice x12, local copies, waits for them, and re-layouts, per_device(): lax.scan(attend, 0, (query_loc.reshape(blocks, BLOCK_TOKENS, heads_q, hea...  12.2 us
  transfers between devices with their start and end apart: 14, of which 8 were waited for; matrix products, arithmetic and copies ran while one was open for 9% of the time, Pallas kernels for 0%

commit v1 on v0

--- a/solution.py
+++ b/solution.py
@@ -22,7 +22,7 @@
 
 def from_root(block, axis, owner):
     block = jnp.where(lax.axis_index(axis) == owner, block, jnp.zeros_like(block))
-    return lax.psum(block, axis)
+    return jnp.sum(lax.all_gather(block, axis), axis=0)
 
 
 def per_device(queries, keys, values, output_gradient, global_blocks, random_blocks):

time: 497 us -> 474 us (0.954)
  waiting for transfers between devices: 204 us -> 179 us
    psum x1 -> x0, waiting for transfers between devices: 47.8 us -> none  [from_root(): return lax.psum(block, axis)]
    all_to_all x1, waiting for transfers between devices: 0.01 us -> 15.9 us  [per_device(): lax.all_to_all(queries, 'head', split_axis=1, concat_axis=0, tiled=True)]
    all_gather x1, waiting for transfers between devices: 0.01 us -> 12.3 us  [per_device(): everything = lax.all_gather(kv_pair, 'seq', axis=1, tiled=True)]
    unnamed x42 -> x40, local copies, waits for them, and re-layouts: 13.2 us -> 15.3 us
  transfers between devices with their start and end apart: 14 -> 15, of which waited for: 8 -> 9; matrix products, arithmetic and copies ran while one was open for 9% -> 10% of each run, Pallas kernels for 0% -> 0%
where the time goes in v1:
time: 474 us; the launch traced here: 471 us
  waiting for transfers between devices  179 us (38%)
  local copies, waits for them, and re-layouts  86.9 us (18%)
  blocking collectives  60.8 us (13%)
  matrix products  46.3 us (10%)
  other arithmetic  39.3 us (8%)
  starting transfers between devices  36.3 us (8%)
  between operations  19.4 us (4%)
    all_to_all x1, blocking collectives, per_device(): lax.all_to_all(query_grad_all, 'head', split_axis=0, concat_axis=1, tiled...  50.3 us
    psum x1, waiting for transfers between devices, per_device(): lax.psum(global_terms.astype(jnp.bfloat16), 'seq').astype(jnp.float32)  49 us
    all_to_all x1, waiting for transfers between devices, per_device(): lax.all_to_all(out_all, 'head', split_axis=0, concat_axis=1, tiled=True)  43.4 us
    all_to_all x1, waiting for transfers between devices, per_device(): lax.all_to_all(output_gradient, 'head', split_axis=1, concat_axis=0, tile...  41.1 us
    all_to_all x1, waiting for transfers between devices, per_device(): lax.all_to_all(queries, 'head', split_axis=1, concat_axis=0, tiled=True)  15.9 us
    unnamed x40, local copies, waits for them, and re-layouts  15.3 us
    dot_general x4, matrix products, attend(): jnp.einsum('qkgd,tbkd->kgqtb', grad_grid, value_t, preferred_element_type...  13 us
    all_gather x1, waiting for transfers between devices, per_device(): everything = lax.all_gather(kv_pair, 'seq', axis=1, tiled=True)  12.3 us
  transfers between devices with their start and end apart: 15, of which 9 were waited for; matrix products, arithmetic and copies ran while one was open for 10% of the time, Pallas kernels for 0%

profile of v1, /device:TPU:0, one launch (start us, length us, event | category | flops | bytes accessed | tf_op | source)
XLA Modules:
  0.0 471.3 jit_solution(17904135037849792967)
XLA Ops:
  8.9 6.3 %all-to-all-start = ((bf16[128,8,128]{2,0,1:T(8,128)(2,1)}), bf16[128,8,128]{2,0,1:T(8,128)(2,1)S(1)}, u32[]{:S(2)}, u32[]{:S(2)}) async-start(bf16[128,8,128]{2,0,1:T(8,128)(2,1)} %copy.306), calls=%async_computation | async-start | bytes 524288 | tf_op jit(solution)/shard_map/all_to_all | solution.py:31
  24.1 3.4 all-to-all-start.1
  37.8 4.3 copy.315
  42.1 3.6 all-to-all-start.3
  45.7 4.3 copy.314
  50.0 41.1 %all-to-all-done.3 = bf16[128,64,128]{2,0,1:T(8,128)(2,1)S(1)} async-done(((bf16[128,64,128]{2,0,1:T(8,128)(2,1)}), bf16[128,64,128]{2,0,1:T(8,128)(2,1)S(1)}, u32[]{:S(2)}, u32[]{:S(2)}) %all-to-all-start.3) | async-done | bytes 2097184 | tf_op jit(solution)/shard_map/all_to_all | solution.py:33
  91.1 4.5 all-to-all-start.2
  111.0 12.3 %all-gather.6.cloned.1.call-done = bf16[2,4096,256]{2,1,0:T(8,128)(2,1)} async-done(((bf16[2,512,256]{2,1,0:T(8,128)(2,1)}), bf16[2,4096,256]{2,1,0:T(8,128)(2,1)}) %all-gather.6.cloned.1.call-update) | async-done | bytes 4194320 | tf_op jit(solution)/shard_map/all_gather | solution.py:88
  127.5 15.9 %all-to-all-done.2 = bf16[128,64,128]{2,0,1:T(8,128)(2,1)} async-done(((bf16[128,64,128]{2,0,1:T(8,128)(2,1)}), bf16[128,64,128]{2,0,1:T(8,128)(2,1)}, u32[]{:S(2)}, u32[]{:S(2)}) %all-to-all-start.2) | async-done | bytes 2097184 | tf_op jit(solution)/shard_map/all_to_all | solution.py:30
  143.4 101.8 %while.16 = (s32[]{:T(128)}, bf16[4,128,16,128]{3,2,1,0:T(8,128)(2,1)}, bf16[4,128,16,128]{3,2,1,0:T(8,128)(2,1)}, f32[4,8,2,128,256]{3,4,1,2,0:T(8,128)}, s32[4...) while((s32[]{:T(128)}, ...), condition=%wide.region_7.8_spmd, body=%wide.region_3.7_spmd.sunk | while | flops 3265259520 | bytes 89202968 | solution.py:170
  158.7 3.2 fusion.115
  184.2 3.2 fusion.115
  209.6 3.2 fusion.115
  235.0 3.2 fusion.115
  245.2 9.1 %copy.322 = f32[4,8,2,128,256]{4,3,2,0,1:T(8,128)} copy(f32[4,8,2,128,256]{3,4,1,2,0:T(8,128)} %get-tuple-element.94) | data formatting | bytes 16777216 | tf_op jit(solution)/shard_map/while | solution.py:170
  259.6 3.7 all-to-all-start.6
  277.2 3.8 scatter-add.9
  281.0 49.0 %all-reduce.5.cloned.1.call-done = bf16[2,2,128,256]{2,3,0,1:T(8,128)(2,1)} async-done(((bf16[2,2,128,256]{2,3,0,1:T(8,128)(2,1)}), bf16[2,2,128,256]{2,3,0,1:T(8,128)(2,1)}) %all-reduce.5.cloned.1.call-update) | async-done | bytes 262160 | tf_op jit(solution)/shard_map/psum | solution.py:201
  338.4 4.6 all-to-all-start.8
  343.1 8.1 %all-to-all-done.8 = bf16[512,2,128]{2,1,0:T(2,128)(2,1)S(1)} async-done(((bf16[512,2,128]{2,1,0:T(2,128)(2,1)}), bf16[512,2,128]{2,1,0:T(2,128)(2,1)S(1)}, u32[]{:S(2)}, u32[]{:S(2)}) %all-to-all-start.8) | async-done | bytes 262176 | tf_op jit(solution)/shard_map/all_to_all | solution.py:232
  351.1 10.4 %all_to_all.137 = bf16[512,2,128]{2,1,0:T(2,128)(2,1)S(1)} all-to-all(bf16[512,2,128]{2,1,0:T(2,128)(2,1)S(1)} %reshape_squeeze.6), channel_id=1, replica_groups=mesh['seq'=8,'head'=4] {'head'}, dimensions={0} | all-to-all | bytes 524288 | tf_op jit(solution)/shard_map/all_to_all | solution.py:231
  361.6 50.3 %all_to_all.138 = bf16[512,16,128]{2,1,0:T(8,128)(2,1)} all-to-all(bf16[512,16,128]{2,1,0:T(8,128)(2,1)S(1)} %bitcast.280), channel_id=1, replica_groups=mesh['seq'=8,'head'=4] {'head'}, dimensions={0} | all-to-all | bytes 4194304 | tf_op jit(solution)/shard_map/all_to_all | solution.py:230
  411.9 3.6 all-to-all-start.4
  419.4 43.4 %all-to-all-done.4 = bf16[512,16,128]{2,1,0:T(8,128)(2,1)S(1)} async-done(((bf16[512,16,128]{2,1,0:T(8,128)(2,1)}), bf16[512,16,128]{2,1,0:T(8,128)(2,1)S(1)}, u32[]{:S(2)}, u32[]{:S(2)}) %all-to-all-start.4) | async-done | bytes 2097184 | tf_op jit(solution)/shard_map/all_to_all | solution.py:229
  (228 shorter events, 153.9 us)
Async XLA Ops:
  7.2 20.4 %copy-start.13 = (s32[2]{0:T(128)S(1)}, s32[2]{0:T(128)}, u32[]{:S(2)}) copy-start(s32[2]{0:T(128)} %param.16) | copy-start | bytes 28
  8.9 15.3 %all-to-all-start = ((bf16[128,8,128]{2,0,1:T(8,128)(2,1)}), bf16[128,8,128]{2,0,1:T(8,128)(2,1)S(1)}, u32[]{:S(2)}, u32[]{:S(2)}) async-start(bf16[128,8,128]{2,0,1:T(8,128)(2,1)} %copy.306), calls=%async_computation | async-start | bytes 524288 | tf_op jit(solution)/shard_map/all_to_all | solution.py:31
  24.1 10.4 %all-to-all-start.1 = ((bf16[128,8,128]{2,0,1:T(8,128)(2,1)}), bf16[128,8,128]{2,0,1:T(8,128)(2,1)S(1)}, u32[]{:S(2)}, u32[]{:S(2)}) async-start(bf16[128,8,128]{2,0,1:T(8,128)(2,1)} %copy.308), calls=%async_computation.1 | async-start | bytes 524288 | tf_op jit(solution)/shard_map/all_to_all | solution.py:32
  27.5 78.1 %all-gather.10.cloned.1.call-start = ((), (), s32[]{:S(2)}) async-start(), calls=%async_computation.12 | async-start | bytes 1179648 | tf_op jit(solution)/shard_map/all_gather | solution.py:25
  35.8 71.2 %all-gather.8.cloned.1.call-start = ((), (), s32[]{:S(2)}) async-start(), calls=%async_computation.11 | async-start | bytes 1179648 | tf_op jit(solution)/shard_map/all_gather | solution.py:25
  36.5 86.8 %all-gather.6.cloned.1.call-start = ((), (), s32[]{:S(2)}) async-start(), calls=%async_computation.9 | async-start | bytes 4718592 | tf_op jit(solution)/shard_map/all_gather | solution.py:88
  42.1 49.0 %all-to-all-start.3 = ((bf16[128,64,128]{2,0,1:T(8,128)(2,1)}), bf16[128,64,128]{2,0,1:T(8,128)(2,1)S(1)}, u32[]{:S(2)}, u32[]{:S(2)}) async-start(bf16[128,64,128]{2,0,1:T(8,128)(2,1)} %copy.315), calls=%async_computation.3 | async-start | bytes 4194304 | tf_op jit(solution)/shard_map/all_to_all | solution.py:33
  50.0 45.7 %copy-start.12 = (s32[32,3]{0,1:T(4,128)S(1)}, s32[32,3]{0,1:T(4,128)}, u32[]{:S(2)}) copy-start(s32[32,3]{0,1:T(4,128)} %param.17) | copy-start | bytes 1156
  50.0 48.4 %copy-start.2 = (bf16[2,512,256]{2,1,0:T(8,128)(2,1)S(1)}, bf16[2,512,256]{2,1,0:T(8,128)(2,1)}, u32[]{:S(2)}) copy-start(bf16[2,512,256]{2,1,0:T(8,128)(2,1)} %copy-done.1) | copy-start | bytes 1572868
  91.1 52.3 %all-to-all-start.2 = ((bf16[128,64,128]{2,0,1:T(8,128)(2,1)}), bf16[128,64,128]{2,0,1:T(8,128)(2,1)}, u32[]{:S(2)}, u32[]{:S(2)}) async-start(bf16[128,64,128]{2,0,1:T(8,128)(2,1)} %copy.314), calls=%async_computation.2 | async-start | bytes 4194304 | tf_op jit(solution)/shard_map/all_to_all | solution.py:30
  97.4 8.2 %copy-start.6 = (s32[8,12]{1,0:T(8,128)}, s32[8,12]{1,0:T(8,128)S(1)}, u32[]{:S(2)}) copy-start(s32[8,12]{1,0:T(8,128)S(1)} %copy.334) | copy-start | bytes 1156
  98.4 3.2 collective-permute-start
  99.7 5.0 %collective-permute-start.1 = (bf16[2,128,256]{2,1,0:T(8,128)(2,1)S(1)}, bf16[2,128,256]{2,1,0:T(8,128)(2,1)S(1)}, u32[]{:S(2)}, u32[]{:S(2)}) collective-permute-start(bf16[2,128,256]{2,1,0:T(8,128)(2,1)S(1)} %get-tuple-element.247), channel_id=1, source_target_pairs={{4,0},{8,4},{12,8},{16,12},{20,16},{24,20},{28,24},{5,1},{9,5},{13... | collective-permute-start | bytes 393224 | tf_op jit(solution)/shard_map/ppermute | solution.py:18
  259.6 3.8 copy-start.14
  259.6 3.9 copy-start.7
  259.6 3.9 copy-start.10
  259.6 3.9 copy-start.15
  259.6 74.6 %all-to-all-start.6 = ((bf16[16,2,128,256]{3,2,1,0:T(8,128)(2,1)}), bf16[16,2,128,256]{3,2,1,0:T(8,128)(2,1)S(1)}, u32[]{:S(2)}, u32[]{:S(2)}) async-start(bf16[16,2,128,256]{3,2,1,0:T(8,128)(2,1)} %copy.338), calls=%async_computation.6 | async-start | bytes 4194304 | tf_op jit(solution)/shard_map/all_to_all | solution.py:216
  263.3 66.6 %all-reduce.5.cloned.1.call-start = ((), (), s32[]{:S(2)}) async-start(), calls=%async_computation.10 | async-start | bytes 524288 | tf_op jit(solution)/shard_map/psum | solution.py:201
  267.3 7.5 %collective-permute-start.2 = (bf16[2,128,256]{2,1,0:T(8,128)(2,1)S(1)}, bf16[2,128,256]{2,1,0:T(8,128)(2,1)S(1)}, u32[]{:S(2)}, u32[]{:S(2)}) collective-permute-start(bf16[2,128,256]{2,1,0:T(8,128)(2,1)S(1)} %get-tuple-element.240), channel_id=1, source_target_pairs={{0,4},{4,8},{8,12},{12,16},{16,20},{20,24},{24,28},{1,5},{5,9},{9,... | collective-permute-start | bytes 393224 | tf_op jit(solution)/shard_map/ppermute | solution.py:17
  269.7 5.2 %collective-permute-start.3 = (bf16[2,128,256]{2,1,0:T(8,128)(2,1)S(1)}, bf16[2,128,256]{2,1,0:T(8,128)(2,1)S(1)}, u32[]{:S(2)}, u32[]{:S(2)}) collective-permute-start(bf16[2,128,256]{2,1,0:T(8,128)(2,1)S(1)} %get-tuple-element.241), channel_id=1, source_target_pairs={{4,0},{8,4},{12,8},{16,12},{20,16},{24,20},{28,24},{5,1},{9,5},{13... | collective-permute-start | bytes 393224 | tf_op jit(solution)/shard_map/ppermute | solution.py:18
  337.4 24.2 %copy-start.3 = (bf16[4,128,16,128]{3,2,1,0:T(8,128)(2,1)S(1)}, bf16[4,128,16,128]{3,2,1,0:T(8,128)(2,1)}, u32[]{:S(2)}) copy-start(bf16[4,128,16,128]{3,2,1,0:T(8,128)(2,1)} %get-tuple-element.93) | copy-start | bytes 6291460
  338.4 12.8 %all-to-all-start.8 = ((bf16[512,2,128]{2,1,0:T(2,128)(2,1)}), bf16[512,2,128]{2,1,0:T(2,128)(2,1)S(1)}, u32[]{:S(2)}, u32[]{:S(2)}) async-start(bf16[512,2,128]{2,1,0:T(2,128)(2,1)} %reshape_squeeze.7), calls=%async_computation.8 | async-start | bytes 524288 | tf_op jit(solution)/shard_map/all_to_all | solution.py:232
  411.9 50.9 %all-to-all-start.4 = ((bf16[512,16,128]{2,1,0:T(8,128)(2,1)}), bf16[512,16,128]{2,1,0:T(8,128)(2,1)S(1)}, u32[]{:S(2)}, u32[]{:S(2)}) async-start(bf16[512,16,128]{2,1,0:T(8,128)(2,1)} %bitcast.281), calls=%async_computation.4 | async-start | bytes 4194304 | tf_op jit(solution)/shard_map/all_to_all | solution.py:229
  (7 other events, 11.1 us)
Sparse Core Ops, SparseCore 0:
  35.9 22.9 all-gather.9
  61.4 23.3 all-gather.7
  86.7 36.5 all-gather.5
  273.6 56.2 all-reduce.4
